TPU v7x, 256 devices: a whole 4x4x8 slice. The times are simulated.
256 devices in a mesh: member: 128 (over y, z_lo, x, core), mp: 2 (over z_hi).
Axes of the slice: x: 4, y: 4, z: 8 (z_hi: 2, z_lo: 4; z = z_hi * 4 + z_lo), core: 2. Of those that a mesh axis runs over, the one named last changes fastest.
Arguments:
- token_ids: int32 [512, 64], P('member'), may hold values from 0 to 76031
- fit_ranks: int32 [512], P('member'), may hold values from 0 to 511, as said below
- embed_table: bfloat16 [3584, 76032], P('member'), may hold values from -40 to 40
- norm_gain: float32 [3584], replicated, may hold values from 0.1 to 1.9
- qkv_weight: bfloat16 [3584, 2304], P('member', 'mp'), may hold values from -0.09375 to 0.09375
- qkv_bias: float32 [2304], P('mp'), may hold values from -3 to 3
- out_weight: bfloat16 [3584, 1792], P('member', 'mp'), may hold values from -0.125 to 0.125
- value_weight: float32 [3584], replicated, may hold values from -0.09375 to 0.09375
- qkv_left: bfloat16 [512, 3584], P('member'), may hold values from -5 to 5
- qkv_right: bfloat16 [512, 2304], P('member', 'mp'), may hold values from -5 to 5
- out_left: bfloat16 [512, 1792], P('member', 'mp'), may hold values from -5 to 5
- out_right: bfloat16 [512, 3584], P('member'), may hold values from -5 to 5
Outputs:
- values: float32 [512, 64], P(('member', 'mp'))
- qkv_grad: float32 [3584, 2304], P('member', 'mp')
- out_grad: float32 [3584, 1792], P('member', 'mp')
Inputs may be any that keep to these rules, and one draw needn't show every extreme that they name: `fit_ranks`: A member's rank is the number of members whose integer fitness score is strictly lower; equal scores share a rank.
All inputs are finite; a program needn't handle non-finite values.
Results may differ from a plain program's by a relative error of at most 0.0052.
Values may be sent and summed in bfloat16 or wider, within the bound.
No kernel may reach another device: no remote copies, remote signals or barrier semaphores. Data moves between devices by JAX's collectives and lax.ppermute only.
A program may use at most 128 MiB of HBM per device.

v0:
```python
import math
import jax
import jax.numpy as jnp
from jax import lax
from jax.sharding import PartitionSpec as P

HD = 128
HQ = 14
HK = 2
SIGMA = 0.01
EPSILON = 1e-06
THETA = 1000000.0
MASKED = -1e30


def rope_tables(length, head_size):
    halfway = head_size // 2
    inverse = THETA ** (-(jnp.arange(halfway, dtype=jnp.float32) * 2.0 / head_size))
    places = jnp.arange(length, dtype=jnp.float32)
    angles = places[:, None] * inverse[None, :]
    angles = jnp.concatenate([angles, angles], axis=1)
    return (jnp.cos(angles), jnp.sin(angles))


def rotate(states, cosine, sine_table):
    halfway = states.shape[-1] // 2
    turned = jnp.concatenate([-states[..., halfway:], states[..., :halfway]], axis=-1)
    return states * cosine[None, :, None, :] + turned * sine_table[None, :, None, :]


def attend(query_heads, key_heads, value_heads, kv_count):
    members, length, head_count, head_size = query_heads.shape
    group_size = head_count // kv_count
    grouped = query_heads.reshape(members, length, kv_count, group_size, head_size)
    scores = jnp.einsum(
        "mskgd,mtkd->mkgst", grouped, key_heads, preferred_element_type=jnp.float32
    ) / math.sqrt(head_size)
    causal = jnp.arange(length)[None, :] <= jnp.arange(length)[:, None]
    scores = jnp.where(causal, scores, MASKED)
    top = jnp.max(scores, axis=-1, keepdims=True)
    weights = jnp.exp(scores - top)
    weights = (weights / jnp.sum(weights, axis=-1, keepdims=True)).astype(jnp.bfloat16)
    context = jnp.einsum(
        "mkgst,mtkd->mskgd", weights, value_heads, preferred_element_type=jnp.float32
    )
    return context.astype(jnp.bfloat16).reshape(members, length, head_count * head_size)


def on_device(
    token_ids,
    fit_ranks,
    embed_table,
    norm_gain,
    qkv_weight,
    qkv_bias,
    out_weight,
    value_weight,
    qkv_left,
    qkv_right,
    out_left,
    out_right,
):
    members, length = token_ids.shape
    row_count = members * length
    mp_size = lax.axis_size("mp")
    heads_here = HQ // mp_size
    kv_here = HK // mp_size
    population = members * lax.axis_size("member")
    contract_rows = (((0,), (0,)), ((), ()))
    contract_cols = (((1,), (1,)), ((), ()))
    all_ids = lax.all_gather(token_ids, "member", axis=0, tiled=True)
    picked = jnp.take(embed_table, all_ids.reshape(-1), axis=1)
    embedded = lax.all_to_all(picked, "member", split_axis=1, concat_axis=0, tiled=True)
    features = embedded.astype(jnp.float32)
    inverse_rms = lax.rsqrt(jnp.mean(features * features, axis=0, keepdims=True) + EPSILON)
    normed = (features * inverse_rms * norm_gain[:, None]).astype(jnp.bfloat16)
    base_proj = lax.dot_general(
        normed,
        lax.all_gather(qkv_weight, "member", axis=0, tiled=True),
        contract_rows,
        preferred_element_type=jnp.float32,
    )
    normed_members = normed.reshape(normed.shape[0], members, length)
    coef_in = jnp.einsum("dms,md->ms", normed_members, qkv_left, preferred_element_type=jnp.float32)
    projected = (
        base_proj.reshape(members, length, -1)
        + SIGMA * coef_in[:, :, None] * qkv_right.astype(jnp.float32)[:, None, :]
        + qkv_bias[None, None, :]
    )
    query_width = heads_here * HD
    kv_width = kv_here * HD
    cosine, sine_table = rope_tables(length, HD)
    query_heads = rotate(
        projected[:, :, :query_width].reshape(members, length, heads_here, HD), cosine, sine_table
    ).astype(jnp.bfloat16)
    key_heads = rotate(
        projected[:, :, query_width : query_width + kv_width].reshape(members, length, kv_here, HD),
        cosine,
        sine_table,
    ).astype(jnp.bfloat16)
    value_heads = (
        projected[:, :, query_width + kv_width :]
        .reshape(members, length, kv_here, HD)
        .astype(jnp.bfloat16)
    )
    context = attend(query_heads, key_heads, value_heads, kv_here)
    coef_out = jnp.einsum("msq,mq->ms", context, out_left, preferred_element_type=jnp.float32)
    flat_context = context.reshape(row_count, query_width)
    share_rows = row_count // mp_size
    partial_out = lax.dot_general(
        flat_context,
        lax.all_gather(out_weight, "member", axis=0, tiled=True),
        contract_cols,
        preferred_element_type=jnp.float32,
    )
    head_term = (
        partial_out.reshape(members, length, -1)
        + SIGMA * coef_out[:, :, None] * out_right.astype(jnp.float32)[:, None, :]
    )
    summed = lax.psum_scatter(
        head_term.reshape(row_count, -1), "mp", scatter_dimension=0, tiled=True
    )
    mp_index = lax.axis_index("mp")
    own_embed = lax.dynamic_slice_in_dim(embedded, mp_index * share_rows, share_rows, 1)
    residual = own_embed.T.astype(jnp.float32) + summed
    inverse_out = lax.rsqrt(jnp.mean(residual * residual, axis=1, keepdims=True) + EPSILON)
    value_rows = jnp.sum(residual * inverse_out * value_weight[None, :], axis=1).reshape(
        members // mp_size, length
    )
    rank_values = fit_ranks.astype(jnp.float32)
    first_sum, second_sum = lax.psum(
        (jnp.sum(rank_values), jnp.sum(rank_values * rank_values)), "member"
    )
    center = first_sum / population
    spread = second_sum / population - center * center
    fit_local = (rank_values - center) * lax.rsqrt(spread + EPSILON)
    fitness = lax.all_gather(fit_local, "member", axis=0, tiled=True)
    left_rows, right_rows = (
        lax.all_to_all(qkv_left, "member", split_axis=1, concat_axis=0, tiled=True),
        lax.all_to_all(out_right, "member", split_axis=1, concat_axis=0, tiled=True),
    )
    right_cols, left_cols = (
        lax.all_gather(qkv_right, "member", axis=0, tiled=True),
        lax.all_gather(out_left, "member", axis=0, tiled=True),
    )
    weighted_in = left_rows.astype(jnp.float32) * fitness[:, None]
    qkv_grad = lax.dot_general(
        weighted_in,
        right_cols.astype(jnp.float32),
        contract_rows,
        precision=lax.Precision.HIGHEST,
        preferred_element_type=jnp.float32,
    ) / (population * SIGMA)
    weighted_out = right_rows.astype(jnp.float32) * fitness[:, None]
    out_grad = lax.dot_general(
        weighted_out,
        left_cols.astype(jnp.float32),
        contract_rows,
        precision=lax.Precision.HIGHEST,
        preferred_element_type=jnp.float32,
    ) / (population * SIGMA)
    return (value_rows, qkv_grad, out_grad)


def solution(mesh):
    placed = (
        P("member", None),
        P("member"),
        P("member", None),
        P(),
        P("member", "mp"),
        P("mp"),
        P("member", "mp"),
        P(),
        P("member", None),
        P("member", "mp"),
        P("member", "mp"),
        P("member", None),
    )
    return jax.shard_map(
        on_device,
        mesh=mesh,
        in_specs=placed,
        out_specs=(P(("member", "mp"), None), P("member", "mp"), P("member", "mp")),
        check_vma=False,
    )
```

profile of v0, /device:TPU:128, one launch (start us, length us, event | category | flops | bytes accessed | tf_op | source)
XLA Modules:
  0.0 1395.1 jit_solution(669175354803693460)
XLA Ops:
  7.2 0.7 all-gather.11.cloned.1.call-update
  7.9 0.7 all-gather.9.cloned.1.call-update
  8.6 187.3 %all-gather = s32[128,4,64]{2,1,0:T(4,128)S(1)} all-gather(s32[1,4,64]{2,1,0:T(4,128)} %bitcast.92), channel_id=1, replica_groups=mesh['member'=128,'mp'=2] {'member'}, dimensions={0}, use_global_device_ids=true | all-gather | bytes 132096 | tf_op jit(solution)/shard_map/all_gather | solution.py:71
  196.0 0.2 reshape.198
  196.3 15.8 %copy.45 = bf16[28,76032]{0,1:T(8,128)(2,1)} copy(bf16[28,76032]{1,0:T(8,128)(2,1)} %param.14) | data formatting | bytes 8515584 | tf_op args[2]
  212.2 118.4 %gather_fusion = bf16[32768,28]{1,0:T(8,128)(2,1)} fusion(bf16[28,76032]{0,1:T(8,128)(2,1)} %copy.45, s32[32768]{0:T(1024)S(1)} %broadcast_clamp_fusion), kind=kCustom, calls=%fused_computation | custom fusion | bytes 3801088 | tf_op jit(solution)/shard_map/jit(_take)/gather | solution.py:72
  330.6 7.6 copy.46
  338.4 1.6 broadcast_select_fusion
  340.0 6.3 all-to-all-start
  346.4 0.7 all-gather.13.cloned.1.call-update
  347.2 0.6 convert_element_type.91
  348.0 50.6 %all-to-all-done = bf16[28,128,256]{2,0,1:T(8,128)(2,1)S(1)} async-done(((bf16[28,128,256]{2,0,1:T(8,128)(2,1)}), bf16[28,128,256]{2,0,1:T(8,128)(2,1)S(1)}, u32[]{:S(2)}, u32[]{:S(2)}) %all-to-all-start) | async-done | bytes 1835040 | tf_op jit(solution)/shard_map/all_to_all | solution.py:73
  398.6 1.5 all_to_all.34
  400.1 0.6 multiply_reduce_fusion
  400.8 3.7 fusion.3
  404.5 3.9 copy.47
  408.4 2.4 bitcast_convert_fusion
  410.9 7.8 reshape.204
  418.7 11.5 multiply_convert_fusion
  430.2 0.6 fusion
  430.8 10.4 reshape.237
  441.2 12.7 reshape.232
  453.9 5.9 fusion.2
  460.2 0.3 slice_negate_fusion
  460.5 0.4 fusion.8
  460.9 0.5 fusion.31
  461.7 0.3 fusion.6
  462.0 0.3 copy.50
  462.4 0.5 dot_general.36
  463.2 6.8 convolution_add_fusion
  469.9 5.1 copy.51
  475.1 0.3 all_to_all.37
  475.4 0.8 copy.53
  476.2 13.0 all-to-all-start.2
  489.2 199.0 %all-gather.4 = bf16[128,4,896]{2,1,0:T(4,128)(2,1)S(1)} all-gather(bf16[1,4,896]{2,1,0:T(4,128)(2,1)S(1)} %bitcast.91), channel_id=1, replica_groups=mesh['member'=128,'mp'=2] {'member'}, dimensions={0}, use_global_device_ids=true | all-gather | bytes 924672 | tf_op jit(solution)/shard_map/all_gather | solution.py:144
  688.2 0.6 convert_reduce_fusion
  688.8 338.7 %all-reduce.1 = (f32[]{:T(128)}, f32[]{:T(128)}) all-reduce(f32[]{:T(128)} %get-tuple-element.4, f32[]{:T(128)} %get-tuple-element.3), channel_id=1, replica_groups=mesh['member'=128,'mp'=2] {'member'}, use_global_device_ids=true, to_apply=%region_9.10 | all-reduce | flops 2 | bytes 16 | tf_op jit(solution)/shard_map/psum | solution.py:131
  1027.6 0.3 all_to_all.35
  1030.5 0.8 copy.52
  1031.3 0.6 dynamic-slice
  1032.5 6.2 all-to-all-start.1
  1039.0 340.7 %all-reduce = f32[512]{0:T(512)S(1)} all-reduce(f32[512]{0:T(512)S(1)} %multiply_dynamic-update-slice_fusion), channel_id=1, replica_groups=mesh['member'=128,'mp'=2] {'member'}, use_global_device_ids=true, to_apply=%add | all-reduce | flops 512 | bytes 4096
  1379.9 1.3 convolution_multiply_fusion.2
  1381.2 2.5 reshape.225
  1383.7 1.5 convolution_multiply_fusion
  1385.2 2.1 multiply_reduce_fusion.2
  1387.4 0.6 multiply_reduce_fusion.1
  1387.9 0.6 reshape.203
  (63 shorter events, 2.1 us)
Async XLA Ops:
  7.2 423.6 %all-gather.11.cloned.1.call-start = ((), (), s32[]{:S(2)}) async-start(), calls=%async_computation.6 | async-start | bytes 7397376 | tf_op jit(solution)/shard_map/all_gather | solution.py:112
  7.9 433.3 %all-gather.9.cloned.1.call-start = ((), (), s32[]{:S(2)}) async-start(), calls=%async_computation.5 | async-start | bytes 9510912 | tf_op jit(solution)/shard_map/all_gather | solution.py:79
  340.0 7.1 copy-start.6
  340.0 7.2 copy-start.3
  340.0 58.6 %all-to-all-start = ((bf16[28,128,256]{2,0,1:T(8,128)(2,1)}), bf16[28,128,256]{2,0,1:T(8,128)(2,1)S(1)}, u32[]{:S(2)}, u32[]{:S(2)}) async-start(bf16[28,128,256]{2,0,1:T(8,128)(2,1)} %broadcast_select_fusion), calls=%async_computation | async-start | bytes 4194304 | tf_op jit(solution)/shard_map/all_to_all | solution.py:73
  346.3 1034.9 %all-gather.13.cloned.1.call-start = ((), (), s32[]{:S(2)}) async-start(), calls=%async_computation.7 | async-start | bytes 1188864 | tf_op jit(solution)/shard_map/all_gather | solution.py:143
  347.1 1038.1 %reduce-scatter.2.cloned.1.call-start = ((), (), s32[]{:S(2)}) async-start(), calls=%async_computation.4 | async-start | bytes 5505024 | tf_op jit(solution)/shard_map/reduce_scatter | solution.py:120
  398.6 2.2 copy-start.4
  418.6 11.5 copy-start.7
  441.2 12.7 copy-start.2
  441.2 12.7 copy-start.11
  461.7 1.2 copy-start.9
  462.0 1.1 copy-start.5
  475.1 213.2 %copy-start.10 = (s32[4]{0:T(128)S(1)}, s32[4]{0:T(128)}, u32[]{:S(2)}) copy-start(s32[4]{0:T(128)} %param.13) | copy-start | bytes 52
  475.1 556.2 %copy-start.12 = (u32[256]{0:T(256)S(1)}, u32[256]{0:T(256)}, u32[]{:S(2)}) copy-start(u32[256]{0:T(256)} %constant.74) | copy-start | bytes 3076
  476.2 556.4 %all-to-all-start.2 = ((bf16[4,128,28]{2,0,1:T(4,128)(2,1)}), bf16[4,128,28]{2,0,1:T(4,128)(2,1)S(1)}, u32[]{:S(2)}, u32[]{:S(2)}) async-start(bf16[4,128,28]{2,0,1:T(4,128)(2,1)} %copy.53), calls=%async_computation.3 | async-start | bytes 262144 | tf_op jit(solution)/shard_map/all_to_all | solution.py:140
  1032.5 347.3 %all-to-all-start.1 = ((bf16[4,128,28]{2,0,1:T(4,128)(2,1)}), bf16[4,128,28]{2,0,1:T(4,128)(2,1)S(1)}, u32[]{:S(2)}, u32[]{:S(2)}) async-start(bf16[4,128,28]{2,0,1:T(4,128)(2,1)} %copy.52), calls=%async_computation.2 | async-start | bytes 262144 | tf_op jit(solution)/shard_map/all_to_all | solution.py:139
  1381.2 4.0 copy-start
  1383.7 3.6 copy-start.8
  1385.2 2.1 copy-start.1
Sparse Core Ops, SparseCore 0:
  9.8 203.6 all-gather.10
  215.4 217.5 all-gather.8
  434.9 196.6 all-gather.12
  634.0 90.6 reduce-scatter.1
where the time goes:
time: 1400 us
  blocking collectives  1070 us (76%)
  local copies, waits for them, and re-layouts  191 us (14%)
  waiting for transfers between devices  52.6 us (4%)
  starting transfers between devices  25.7 us (2%)
  other arithmetic  25.4 us (2%)
  between operations  17.4 us (1%)
  matrix products  17.2 us (1%)
    unnamed x1, blocking collectives  341 us
    psum x1, blocking collectives, on_device(): lax.psum((jnp.sum(rank_values), jnp.sum(rank_values * rank_values)), 'mem...  339 us
    all_gather x1, blocking collectives, on_device(): lax.all_gather(out_left, 'member', axis=0, tiled=True)  199 us
    all_gather x1, blocking collectives, on_device(): all_ids = lax.all_gather(token_ids, 'member', axis=0, tiled=True)  187 us
    gather x2, local copies, waits for them, and re-layouts, on_device(): picked = jnp.take(embed_table, all_ids.reshape(-1), axis=1)  126 us
    all_to_all x1, waiting for transfers between devices, on_device(): lax.all_to_all(picked, 'member', split_axis=1, concat_axis=0, tiled=True)  50.6 us
    unnamed x33, local copies, waits for them, and re-layouts  42.2 us
  transfers between devices with their start and end apart: 7, of which 1 were waited for; matrix products, arithmetic and copies ran while one was open for 16% of the time, Pallas kernels for 0%

commit v1 on v0

--- a/solution.py
+++ b/solution.py
@@ -141,7 +141,9 @@
     )
     right_cols, left_cols = (
         lax.all_gather(qkv_right, "member", axis=0, tiled=True),
-        lax.all_gather(out_left, "member", axis=0, tiled=True),
+        jnp.concatenate(
+            lax.all_to_all(jnp.stack([out_left] * lax.axis_size("member")), "member", 0, 0), axis=0
+        ),
     )
     weighted_in = left_rows.astype(jnp.float32) * fitness[:, None]
     qkv_grad = lax.dot_general(

time: 1400 us -> 1240 us (0.89)
  blocking collectives: 1070 us -> 895 us
    all_gather x1 -> x0, blocking collectives: 199 us -> none  [on_device(): lax.all_gather(out_left, 'member', axis=0, tiled=True)]
    psum x1, blocking collectives: 339 us -> 358 us  [on_device(): lax.psum((jnp.sum(rank_values), jnp.sum(rank_values * rank_values)), 'mem...]
    all_to_all x0 -> x1, blocking collectives: none -> 16.4 us  [on_device(): lax.all_to_all(out_right, 'member', split_axis=1, concat_axis=0, tiled=True)]
    unnamed x33 -> x32, local copies, waits for them, and re-layouts: 42.2 us -> 42 us
  transfers between devices with their start and end apart: 7 -> 7, of which waited for: 1 -> 2; matrix products, arithmetic and copies ran while one was open for 16% -> 19% of each run, Pallas kernels for 0% -> 0%
where the time goes in v1:
time: 1240 us; the launch traced here: 1230 us
  blocking collectives  895 us (72%)
  local copies, waits for them, and re-layouts  191 us (15%)
  waiting for transfers between devices  62.8 us (5%)
  starting transfers between devices  25.7 us (2%)
  other arithmetic  25.6 us (2%)
  between operations  17.4 us (1%)
  matrix products  17.1 us (1%)
    psum x1, blocking collectives, on_device(): lax.psum((jnp.sum(rank_values), jnp.sum(rank_values * rank_values)), 'mem...  358 us
    unnamed x1, blocking collectives  333 us
    all_gather x1, blocking collectives, on_device(): all_ids = lax.all_gather(token_ids, 'member', axis=0, tiled=True)  187 us
    gather x2, local copies, waits for them, and re-layouts, on_device(): picked = jnp.take(embed_table, all_ids.reshape(-1), axis=1)  126 us
    all_to_all x1, waiting for transfers between devices, on_device(): lax.all_to_all(picked, 'member', split_axis=1, concat_axis=0, tiled=True)  50.6 us
    unnamed x32, local copies, waits for them, and re-layouts  42 us
  transfers between devices with their start and end apart: 7, of which 2 were waited for; matrix products, arithmetic and copies ran while one was open for 19% of the time, Pallas kernels for 0%

profile of v1, /device:TPU:128, one launch (start us, length us, event | category | flops | bytes accessed | tf_op | source)
XLA Modules:
  0.0 1234.9 jit_solution(1875016032741504963)
XLA Ops:
  7.2 0.7 all-gather.10.cloned.1.call-update
  7.9 0.7 all-gather.8.cloned.1.call-update
  8.6 187.3 %all-gather = s32[128,4,64]{2,1,0:T(4,128)S(1)} all-gather(s32[1,4,64]{2,1,0:T(4,128)} %bitcast.91), channel_id=1, replica_groups=mesh['member'=128,'mp'=2] {'member'}, dimensions={0}, use_global_device_ids=true | all-gather | bytes 132096 | tf_op jit(solution)/shard_map/all_gather | solution.py:71
  196.3 15.8 %copy.48 = bf16[28,76032]{0,1:T(8,128)(2,1)} copy(bf16[28,76032]{1,0:T(8,128)(2,1)} %param.14) | data formatting | bytes 8515584 | tf_op args[2]
  212.2 118.4 %gather_fusion = bf16[32768,28]{1,0:T(8,128)(2,1)} fusion(bf16[28,76032]{0,1:T(8,128)(2,1)} %copy.48, s32[32768]{0:T(1024)S(1)} %broadcast_clamp_fusion), kind=kCustom, calls=%fused_computation | custom fusion | bytes 3801088 | tf_op jit(solution)/shard_map/jit(_take)/gather | solution.py:72
  330.6 7.6 copy.49
  338.4 1.6 broadcast_select_fusion
  340.0 6.3 all-to-all-start
  346.4 0.7 all-gather.12.cloned.1.call-update
  347.2 0.6 convert_element_type.89
  348.0 50.6 %all-to-all-done = bf16[28,128,256]{2,0,1:T(8,128)(2,1)S(1)} async-done(((bf16[28,128,256]{2,0,1:T(8,128)(2,1)}), bf16[28,128,256]{2,0,1:T(8,128)(2,1)S(1)}, u32[]{:S(2)}, u32[]{:S(2)}) %all-to-all-start) | async-done | bytes 1835040 | tf_op jit(solution)/shard_map/all_to_all | solution.py:73
  398.6 1.5 all_to_all.37
  400.1 0.6 multiply_reduce_fusion
  400.8 3.7 fusion.3
  404.5 3.9 copy.50
  408.4 2.4 bitcast_convert_fusion
  410.9 7.8 reshape.210
  418.7 11.5 multiply_convert_fusion
  430.2 0.6 fusion
  430.8 10.4 reshape.240
  441.2 12.7 %reshape.235 = bf16[3584,1152,1]{1,0,2:T(8,128)(2,1)} reshape(bf16[128,28,1152]{2,1,0:T(8,128)(2,1)} %all-gather.8.cloned.1.call-done) | data formatting | bytes 16515072
  453.9 5.9 fusion.2
  460.2 0.3 slice_negate_fusion
  460.5 0.4 fusion.9
  460.9 0.5 fusion.32
  461.7 0.3 fusion.6
  462.0 0.3 copy.53
  462.4 0.5 dot_general.36
  463.2 6.8 convolution_add_fusion
  469.9 5.1 copy.54
  475.1 0.3 all_to_all.38
  475.4 0.8 copy.55
  476.2 13.0 %all-to-all-start.1 = ((bf16[4,128,28]{2,0,1:T(4,128)(2,1)}), bf16[4,128,28]{2,0,1:T(4,128)(2,1)S(1)}, u32[]{:S(2)}, u32[]{:S(2)}) async-start(bf16[4,128,28]{2,0,1:T(4,128)(2,1)} %copy.55), calls=%async_computation.2 | async-start | bytes 262144 | tf_op jit(solution)/shard_map/all_to_all | solution.py:139
  489.2 0.3 all_to_all.40
  489.7 10.1 all-to-all-done.1
  499.8 16.4 %all_to_all.47 = bf16[4,128,28]{2,0,1:T(4,128)(2,1)S(1)} all-to-all(bf16[4,128,28]{2,0,1:T(4,128)(2,1)S(1)} %copy.56), channel_id=1, replica_groups=mesh['member'=128,'mp'=2] {'member'}, dimensions={1} | all-to-all | bytes 57344 | tf_op jit(solution)/shard_map/all_to_all | solution.py:140
  516.2 1.2 stack.2
  517.4 6.2 all-to-all-start.3
  523.6 0.6 convert_reduce_fusion
  524.2 357.8 %all-reduce.1 = (f32[]{:T(128)}, f32[]{:T(128)}) all-reduce(f32[]{:T(128)} %get-tuple-element.4, f32[]{:T(128)} %get-tuple-element.3), channel_id=1, replica_groups=mesh['member'=128,'mp'=2] {'member'}, use_global_device_ids=true, to_apply=%region_9.10 | all-reduce | flops 2 | bytes 16 | tf_op jit(solution)/shard_map/psum | solution.py:131
  884.6 0.6 dynamic-slice
  886.0 333.4 %all-reduce = f32[512]{0:T(512)S(1)} all-reduce(f32[512]{0:T(512)S(1)} %multiply_dynamic-update-slice_fusion), channel_id=1, replica_groups=mesh['member'=128,'mp'=2] {'member'}, use_global_device_ids=true, to_apply=%add | all-reduce | flops 512 | bytes 4096
  1219.8 1.2 fusion.7
  1221.0 2.5 reshape.230
  1223.5 1.5 convolution_multiply_fusion
  1225.0 2.1 multiply_reduce_fusion.2
  1227.1 0.6 multiply_reduce_fusion.1
  1227.7 0.6 reshape.209
  (64 shorter events, 2.5 us)
Async XLA Ops:
  7.2 423.6 %all-gather.10.cloned.1.call-start = ((), (), s32[]{:S(2)}) async-start(), calls=%async_computation.7 | async-start | bytes 7397376 | tf_op jit(solution)/shard_map/all_gather | solution.py:112
  7.9 433.3 %all-gather.8.cloned.1.call-start = ((), (), s32[]{:S(2)}) async-start(), calls=%async_computation.6 | async-start | bytes 9510912 | tf_op jit(solution)/shard_map/all_gather | solution.py:79
  340.0 7.1 copy-start.6
  340.0 7.2 copy-start.3
  340.0 58.6 %all-to-all-start = ((bf16[28,128,256]{2,0,1:T(8,128)(2,1)}), bf16[28,128,256]{2,0,1:T(8,128)(2,1)S(1)}, u32[]{:S(2)}, u32[]{:S(2)}) async-start(bf16[28,128,256]{2,0,1:T(8,128)(2,1)} %broadcast_select_fusion), calls=%async_computation | async-start | bytes 4194304 | tf_op jit(solution)/shard_map/all_to_all | solution.py:73
  346.3 874.6 %all-gather.12.cloned.1.call-start = ((), (), s32[]{:S(2)}) async-start(), calls=%async_computation.8 | async-start | bytes 1188864 | tf_op jit(solution)/shard_map/all_gather | solution.py:143
  347.1 877.9 %reduce-scatter.2.cloned.1.call-start = ((), (), s32[]{:S(2)}) async-start(), calls=%async_computation.5 | async-start | bytes 5505024 | tf_op jit(solution)/shard_map/reduce_scatter | solution.py:120
  398.6 2.2 copy-start.4
  418.6 11.5 copy-start.7
  441.2 12.7 %copy-start.2 = (bf16[256,3584]{1,0:T(8,128)(2,1)S(1)}, bf16[256,3584]{1,0:T(8,128)(2,1)}, u32[]{:S(2)}) copy-start(bf16[256,3584]{1,0:T(8,128)(2,1)} %copy.50) | copy-start | bytes 5505028
  441.2 12.7 %copy-start.11 = (f32[1152]{0:T(1024)S(1)}, f32[1152]{0:T(1024)}, u32[]{:S(2)}) copy-start(f32[1152]{0:T(1024)} %param.17) | copy-start | bytes 13828
  461.7 1.2 copy-start.9
  462.0 1.1 copy-start.5
  475.1 48.5 %copy-start.10 = (s32[4]{0:T(128)S(1)}, s32[4]{0:T(128)}, u32[]{:S(2)}) copy-start(s32[4]{0:T(128)} %param.13) | copy-start | bytes 52
  475.1 409.5 %copy-start.12 = (u32[256]{0:T(256)S(1)}, u32[256]{0:T(256)}, u32[]{:S(2)}) copy-start(u32[256]{0:T(256)} %constant.74) | copy-start | bytes 3076
  476.2 23.6 %all-to-all-start.1 = ((bf16[4,128,28]{2,0,1:T(4,128)(2,1)}), bf16[4,128,28]{2,0,1:T(4,128)(2,1)S(1)}, u32[]{:S(2)}, u32[]{:S(2)}) async-start(bf16[4,128,28]{2,0,1:T(4,128)(2,1)} %copy.55), calls=%async_computation.2 | async-start | bytes 262144 | tf_op jit(solution)/shard_map/all_to_all | solution.py:139
  517.4 702.4 %all-to-all-start.3 = ((bf16[128,4,896]{2,1,0:T(4,128)(2,1)}), bf16[128,4,896]{2,1,0:T(4,128)(2,1)S(1)}, u32[]{:S(2)}, u32[]{:S(2)}) async-start(bf16[128,4,896]{2,1,0:T(4,128)(2,1)} %stack.2), calls=%async_computation.4 | async-start | bytes 1835008 | tf_op jit(solution)/shard_map/all_to_all | solution.py:145
  1221.0 4.0 copy-start
  1223.5 3.6 copy-start.8
  1225.0 2.1 copy-start.1
Sparse Core Ops, SparseCore 0:
  9.8 203.6 all-gather.9
  215.4 217.5 all-gather.7
  434.9 198.6 all-gather.11
  635.9 90.8 reduce-scatter.1
